TPU v7x, 32 devices: a whole 2x2x4 slice. The times are simulated.
32 devices in a mesh: uv: 8 (over y, x, core), chan: 4 (over z).
Axes of the slice: x: 2, y: 2, z: 4, core: 2. Of those that a mesh axis runs over, the one named last changes fastest.
Arguments:
- vis: bfloat16 [98304, 2, 1024], P('uv', None, 'chan'), may hold values from -6 to 6
- row_cell: int32 [98304], P('uv'), may hold values from 0 to 127
- tap_weight: bfloat16 [8, 98304], P(None, 'uv'), may hold values from 0.029907227 to 0.29882812
- tap_offset: int32 [8], replicated, may hold values from -32 to 32
- block_tile: int32 [768], P('uv'), may hold values from 0 to 79, as said below
- tile_owner: int32 [80], replicated, may hold values from 0 to 7, as said below
- galaxy: bfloat16 [152, 128, 2048], P('uv', 'chan'), may hold values from -6 to 6
Outputs:
- delay_cube: bfloat16 [152, 128, 2048], P('uv', 'chan')
- cross_power: float32 [152, 1024], P('uv')
Inputs may be any that keep to these rules, and one draw needn't show every extreme that they name: `tile_owner`: each of the 8 owners holds 1 to 19 tiles, and some owner exactly 19. `block_tile`: of the 96 row blocks of one index of uv, at most 22 lie in tiles of one owner, and exactly 22 lie in the tiles of some owner.
All inputs are finite; a program needn't handle non-finite values.
Results may differ from a plain program's by a relative error of at most 0.0059.
Values may be sent and summed in bfloat16 or wider, within the bound.
No kernel may reach another device: no remote copies, remote signals or barrier semaphores. Data moves between devices by JAX's collectives and lax.ppermute only.
A program may use at most 128 MiB of HBM per device.

v0:
```python
import math
import jax
import jax.numpy as jnp
from jax import lax
from jax.sharding import PartitionSpec as P

CH = 1024
BR = 128
TC = 128
KT = 8
TILES_DEV = 10


def tile_ranks(tile_owner, owners):
    onehot = (tile_owner[:, None] == jnp.arange(owners, dtype=jnp.int32)[None, :]).astype(jnp.int32)
    before = jnp.cumsum(onehot, axis=0) - onehot
    return jnp.sum(before * onehot, axis=1)


def kernel_matrix(cells, weights, tap_offset):
    positions = jnp.arange(TC, dtype=jnp.int32)
    total = jnp.zeros(cells.shape[:-1] + (TC, cells.shape[-1]), jnp.float32)
    for k in range(KT):
        target = cells + tap_offset[k]
        hit = target[..., None, :] == positions[:, None]
        total = total + jnp.where(
            hit, weights[..., k, :].astype(jnp.float32)[..., None, :], jnp.float32(0.0)
        )
    return total.astype(jnp.bfloat16)


def delay_table():
    freq = jnp.arange(CH, dtype=jnp.int32)
    phase = (freq[:, None] * freq[None, :] % CH).astype(jnp.float32) * jnp.float32(
        2.0 * math.pi / CH
    )
    cosine = jnp.cos(phase)
    sine = jnp.sin(phase)
    x = freq.astype(jnp.float32) * jnp.float32(2.0 * math.pi / CH)
    taper = 0.35875 - 0.48829 * jnp.cos(x) + 0.14128 * jnp.cos(2.0 * x) - 0.01168 * jnp.cos(3.0 * x)
    scale = (taper / jnp.float32(math.sqrt(CH)))[:, None]
    upper = jnp.concatenate([cosine * scale, -sine * scale], axis=1)
    lower = jnp.concatenate([sine * scale, cosine * scale], axis=1)
    return jnp.concatenate([upper, lower], axis=0).astype(jnp.bfloat16)


def body(vis, row_cell, tap_weight, tap_offset, block_tile, tile_owner, galaxy):
    n_owners = lax.axis_size("uv")
    nblocks = block_tile.shape[0]
    mean_load = nblocks // n_owners
    capacity = mean_load + (TILES_DEV - 1) * mean_load // TILES_DEV
    slots_dev = 2 * TILES_DEV - 1
    chan_dev = vis.shape[2]
    buffer_size = n_owners * capacity
    rank_of_tile = tile_ranks(tile_owner, n_owners)
    target_owner = tile_owner[block_tile]
    owner_hot = (target_owner[:, None] == jnp.arange(n_owners, dtype=jnp.int32)[None, :]).astype(
        jnp.int32
    )
    earlier = jnp.cumsum(owner_hot, axis=0) - owner_hot
    place = target_owner * capacity + jnp.sum(earlier * owner_hot, axis=1)
    blocks = vis.reshape(nblocks, BR, 2 * chan_dev)
    cells = row_cell.reshape(nblocks, BR)
    weights = jnp.transpose(tap_weight.reshape(KT, nblocks, BR), (1, 0, 2))
    sent_vis = jnp.zeros((buffer_size, BR, 2 * chan_dev), jnp.bfloat16).at[place].set(blocks)
    sent_tile = jnp.full((buffer_size,), -1, jnp.int32).at[place].set(block_tile)
    sent_cells = jnp.zeros((buffer_size, BR), jnp.int32).at[place].set(cells)
    sent_weights = jnp.zeros((buffer_size, KT, BR), jnp.bfloat16).at[place].set(weights)
    got_vis, got_tile, got_cells, got_weights = (
        lax.all_to_all(sent_vis, "uv", split_axis=0, concat_axis=0, tiled=True),
        lax.all_to_all(sent_tile, "uv", split_axis=0, concat_axis=0, tiled=True),
        lax.all_to_all(sent_cells, "uv", split_axis=0, concat_axis=0, tiled=True),
        lax.all_to_all(sent_weights, "uv", split_axis=0, concat_axis=0, tiled=True),
    )
    got_matrix = kernel_matrix(got_cells, got_weights, tap_offset)
    contrib = jnp.einsum("bcr,brf->bcf", got_matrix, got_vis, preferred_element_type=jnp.float32)
    slot = jnp.where(got_tile >= 0, rank_of_tile[jnp.maximum(got_tile, 0)], -1)
    pick = (slot[:, None] == jnp.arange(slots_dev, dtype=jnp.int32)[None, :]).astype(jnp.float32)
    grid = jnp.einsum("bs,bcf->scf", pick, contrib, precision=lax.Precision.HIGHEST)
    gridded = grid.astype(jnp.bfloat16).reshape(slots_dev, TC, 2, chan_dev)
    table = delay_table()
    piece = lax.all_to_all(gridded, "chan", split_axis=1, concat_axis=3, tiled=True)
    count = piece.shape[0]
    cells_part = piece.shape[1]
    flat = piece.reshape(count * cells_part, 2 * CH)
    out = jnp.dot(flat, table, preferred_element_type=jnp.float32)
    delay = out.reshape(count, cells_part, 2 * CH)
    galaxy_f = galaxy.astype(jnp.float32)
    product = delay[..., :CH] * galaxy_f[..., :CH] + delay[..., CH:] * galaxy_f[..., CH:]
    local_power = jnp.sum(product, axis=1)
    power = lax.psum(local_power, "chan") / jnp.float32(math.sqrt(TC))
    return (delay.astype(jnp.bfloat16), power)


def solution(mesh):
    return jax.shard_map(
        body,
        mesh=mesh,
        in_specs=(
            P("uv", None, "chan"),
            P("uv"),
            P(None, "uv"),
            P(),
            P("uv"),
            P(),
            P("uv", "chan", None),
        ),
        out_specs=(P("uv", "chan", None), P("uv", None)),
        check_vma=False,
    )
```

profile of v0, /device:TPU:0, one launch (start us, length us, event | category | flops | bytes accessed | tf_op | source)
XLA Modules:
  0.0 569.6 jit_solution(16998166635543470072)
XLA Ops:
  7.9 1.6 gather_fusion
  9.9 1.0 scatter_custom_fusion
  10.9 0.7 all_to_all.29
  11.6 5.2 all-to-all-start
  16.8 0.8 scatter_custom_fusion.1
  18.2 3.1 all-to-all-done
  21.4 3.4 all-to-all-start.1
  24.7 0.8 broadcast_in_dim.144
  25.5 10.6 %scatter_fusion = bf16[176,8,128]{2,1,0:T(8,128)(2,1)} fusion(bf16[176,8,128]{2,1,0:T(8,128)(2,1)} %broadcast_in_dim.144, s32[96]{0:T(128)S(1)} %fusion.47, bf16[96,8,128]{2,1,0:T(8,128)(2,1)} %bitcast.45), kind=kCustom, calls=%fused_computation.4 | custom fusion | bytes 590208 | tf_op jit(solution)/shard_map/scatter | solution.py:68
  36.1 4.1 all-to-all-start.2
  40.3 20.5 %reshape.204 = bf16[96,128,512]{2,1,0:T(8,128)(2,1)} reshape(bf16[12288,2,256]{2,1,0:T(2,128)(2,1)} %param.7) | data formatting | bytes 25165824 | tf_op jit(solution)/shard_map/reshape | solution.py:62
  60.7 7.9 %broadcast_in_dim.170 = bf16[176,128,512]{2,1,0:T(8,128)(2,1)} broadcast(bf16[]{:T(256)} %constant.24.clone.1), dimensions={} | broadcast | bytes 23068674 | tf_op jit(solution)/shard_map/broadcast_in_dim | solution.py:65
  68.6 33.0 %scatter_fusion.1 = bf16[176,128,512]{2,1,0:T(8,128)(2,1)} fusion(bf16[176,128,512]{2,1,0:T(8,128)(2,1)} %broadcast_in_dim.170, s32[96]{0:T(128)S(1)} %fusion.47, bf16[96,128,512]{2,1,0:T(8,128)(2,1)} %reshape.204), kind=kCustom, calls=%fused_computation.5 | custom fusion | bytes 37749120 | tf_op jit(solution)/shard_map/scatter | solution.py:65
  101.6 6.4 %all-to-all-start.3 = ((bf16[176,128,512]{2,1,0:T(8,128)(2,1)}), bf16[176,128,512]{2,1,0:T(8,128)(2,1)}, u32[]{:S(2)}, u32[]{:S(2)}) async-start(bf16[176,128,512]{2,1,0:T(8,128)(2,1)} %scatter_fusion.1), calls=%async_computation.3 | async-start | bytes 46137344 | tf_op jit(solution)/shard_map/all_to_all | solution.py:70
  108.3 0.7 fusion.52
  109.3 1.6 gather_fusion.1
  110.9 5.1 broadcast_add_fusion.7
  116.6 242.7 %all-to-all-done.3 = bf16[176,128,512]{2,1,0:T(8,128)(2,1)} async-done(((bf16[176,128,512]{2,1,0:T(8,128)(2,1)}), bf16[176,128,512]{2,1,0:T(8,128)(2,1)}, u32[]{:S(2)}, u32[]{:S(2)}) %all-to-all-start.3) | async-done | bytes 23068704 | tf_op jit(solution)/shard_map/all_to_all | solution.py:70
  359.4 29.0 %fusion.9 = f32[176,128,512]{2,1,0:T(8,128)} fusion(bf16[176,128,512]{2,1,0:T(8,128)(2,1)} %all-to-all-done.3, f32[176,128]{1,0:T(8,128)S(1)} %bitcast.47, s32[176,128]{1,0:T(8,128)S(1)} %add.223, f32[176,128]{1,0:T(8,128)S(1)} %bitcast.48, s32[176,128]{1,0:T(8,128)S(1)} %add.219, f32[176,128]{1,0:T(8,128)S(1)} %bitcast.49, s32[176,128]{1,0:T(8,128)S(1)} %add.215, ...), kind=kOutput, calls=%fused_computation.28 | convolution fusion | flops 3021996032 | bytes 70647808 | tf_op jit(solution)/shard_map/bcr,brf->bcf/dot_general | solution.py:76
  388.4 49.7 %fusion.35 = bf16[19,128,512]{2,0,1:T(8,128)(2,1)S(1)} fusion(f32[176,128,512]{2,1,0:T(8,128)} %fusion.9, s32[176]{0:T(256)S(1)} %broadcast_select_fusion), kind=kOutput, calls=%fused_computation.59 | convolution fusion | flops 2631077120 | bytes 48628416 | tf_op jit(solution)/shard_map/bs,bcf->scf/dot_general | solution.py:79
  438.1 3.4 copy.18
  441.5 7.4 %copy.19 = bf16[19,128,2,256]{3,2,0,1:T(2,128)(2,1)} copy(bf16[19,128,2,256]{1,3,2,0:T(8,128)(2,1)} %bitcast.43) | data formatting | bytes 4980736 | tf_op jit(solution)/shard_map/reshape | solution.py:80
  448.9 4.9 all-to-all-start.4
  453.8 4.6 convert_element_type.65
  458.4 19.1 %multiply_convert_fusion.1 = (bf16[1024,1024]{1,0:T(8,128)(2,1)}, bf16[1024,1024]{1,0:T(8,128)(2,1)}, bf16[1024,1024]{1,0:T(8,128)(2,1)}) fusion(f32[1024]{0:T(1024)S(1)} %subtract_multiply_fusion), kind=kLoop, calls=%fused_computation.50 | loop fusion | flops 22020096 | bytes 6295552 | tf_op jit(solution)/shard_map/convert.13
  477.5 30.1 %all-to-all-done.4 = bf16[19,128,2,256]{3,2,0,1:T(2,128)(2,1)S(1)} async-done(((bf16[19,128,2,256]{3,2,0,1:T(2,128)(2,1)}), bf16[19,128,2,256]{3,2,0,1:T(2,128)(2,1)S(1)}, u32[]{:S(2)}, u32[]{:S(2)}) %all-to-all-start.4) | async-done | bytes 2490400 | tf_op jit(solution)/shard_map/all_to_all | solution.py:82
  508.1 2.2 copy.21
  510.2 3.0 dot_general.13
  513.3 11.1 %fusion.53 = (bf16[19,32,2048]{2,1,0:T(8,128)(2,1)}, f32[19,32,2048]{2,1,0:T(8,128)S(1)}) fusion(bf16[19,32,2048]{2,1,0:T(8,128)(2,1)} %dot_general.13, bf16[1024,1024]{1,0:T(8,128)(2,1)} %get-tuple-element.20, bf16[1024,1024]{1,0:T(8,128)(2,1)} %get-tuple-element.19, bf16[1024,1024]{1,0:T(8,128)(2,1)} %get-tuple-element.18), kind=kOutput, calls=%fused_computation.104 | convolution fusion | flops 5135073280 | bytes 16252928 | tf_op jit(solution)/shard_map/dot_general | solution.py:86
  524.3 2.0 fusion.34
  526.4 34.8 %all-reduce.2.cloned.1.call-done = f32[19,1024]{1,0:T(8,128)} async-done(((f32[19,1024]{1,0:T(8,128)}), f32[19,1024]{1,0:T(8,128)}) %all-reduce.2.cloned.1.call-update) | async-done | bytes 77840 | tf_op jit(solution)/shard_map/psum | solution.py:91
  561.2 1.5 broadcast_multiply_fusion
  (44 shorter events, 3.4 us)
Async XLA Ops:
  7.2 9.6 %copy-start = (s32[12288]{0:T(1024)S(1)}, s32[12288]{0:T(1024)}, u32[]{:S(2)}) copy-start(s32[12288]{0:T(1024)} %param.8) | copy-start | bytes 147460
  11.6 9.8 %all-to-all-start = ((s32[8,22,1]{1,2,0:T(1,128)}), s32[8,22,1]{1,2,0:T(1,128)S(1)}, u32[]{:S(2)}, u32[]{:S(2)}) async-start(s32[8,22,1]{1,2,0:T(1,128)} %bitcast.2), calls=%async_computation | async-start | bytes 8192 | tf_op jit(solution)/shard_map/all_to_all | solution.py:71
  21.4 14.8 %all-to-all-start.1 = ((s32[8,22,128]{2,1,0:T(8,128)}), s32[8,22,128]{2,1,0:T(8,128)S(1)}, u32[]{:S(2)}, u32[]{:S(2)}) async-start(s32[8,22,128]{2,1,0:T(8,128)} %all_to_all.31), calls=%async_computation.1 | async-start | bytes 196608 | tf_op jit(solution)/shard_map/all_to_all | solution.py:72
  36.1 65.5 %all-to-all-start.2 = ((bf16[176,8,128]{2,1,0:T(8,128)(2,1)}), bf16[176,8,128]{2,1,0:T(8,128)(2,1)S(1)}, u32[]{:S(2)}, u32[]{:S(2)}) async-start(bf16[176,8,128]{2,1,0:T(8,128)(2,1)} %scatter_fusion), calls=%async_computation.2 | async-start | bytes 720896 | tf_op jit(solution)/shard_map/all_to_all | solution.py:73
  101.6 6.5 %copy-start.2 = (s32[80]{0:T(128)S(1)}, s32[80]{0:T(128)}, u32[]{:S(2)}) copy-start(s32[80]{0:T(128)} %param.12) | copy-start | bytes 964
  101.6 6.7 %copy-start.3 = (s32[8]{0:T(128)S(1)}, s32[8]{0:T(128)}, u32[]{:S(2)}) copy-start(s32[8]{0:T(128)} %param.10) | copy-start | bytes 100
  101.6 257.8 %all-to-all-start.3 = ((bf16[176,128,512]{2,1,0:T(8,128)(2,1)}), bf16[176,128,512]{2,1,0:T(8,128)(2,1)}, u32[]{:S(2)}, u32[]{:S(2)}) async-start(bf16[176,128,512]{2,1,0:T(8,128)(2,1)} %scatter_fusion.1), calls=%async_computation.3 | async-start | bytes 46137344 | tf_op jit(solution)/shard_map/all_to_all | solution.py:70
  448.9 58.7 %all-to-all-start.4 = ((bf16[19,128,2,256]{3,2,0,1:T(2,128)(2,1)}), bf16[19,128,2,256]{3,2,0,1:T(2,128)(2,1)S(1)}, u32[]{:S(2)}, u32[]{:S(2)}) async-start(bf16[19,128,2,256]{3,2,0,1:T(2,128)(2,1)} %copy.19), calls=%async_computation.4 | async-start | bytes 4980736 | tf_op jit(solution)/shard_map/all_to_all | solution.py:82
  453.8 107.4 %all-reduce.2.cloned.1.call-start = ((), (), s32[]{:S(2)}) async-start(), calls=%async_computation.5 | async-start | bytes 196608 | tf_op jit(solution)/shard_map/psum | solution.py:91
  510.2 14.1 %slice-start = ((s8[4980736]{0:T(1024)(128)(4,1)}), s8[786432]{0:T(1024)(128)(4,1)S(1)}, s32[]{:S(2)}) async-start(s8[4980736]{0:T(1024)(128)(4,1)} %bitcast.41), calls=%async_computation.6 | async-start | bytes 1572864
  513.3 11.1 %slice-start.1 = ((s8[4980736]{0:T(1024)(128)(4,1)}), s8[4194304]{0:T(1024)(128)(4,1)S(1)}, s32[]{:S(2)}) async-start(s8[4980736]{0:T(1024)(128)(4,1)} %bitcast.41), calls=%async_computation.7 | async-start | bytes 8388608
  513.3 49.4 %copy-start.1 = (s32[12288]{0:T(1024)S(1)}, s32[12288]{0:T(1024)}, u32[]{:S(2)}) copy-start(s32[12288]{0:T(1024)} %param.8) | copy-start | bytes 147460
Sparse Core Ops, SparseCore 0:
  526.5 34.6 all-reduce.1
where the time goes:
time: 572 us; the launch traced here: 570 us
  waiting for transfers between devices  311 us (54%)
  local copies, waits for them, and re-layouts  96.4 us (17%)
  matrix products  89.8 us (16%)
  other arithmetic  34.3 us (6%)
  starting transfers between devices  24 us (4%)
  between operations  14.3 us (2%)
    all_to_all x1, waiting for transfers between devices, body(): lax.all_to_all(sent_vis, 'uv', split_axis=0, concat_axis=0, tiled=True)  243 us
    dot_general x1, matrix products, body(): jnp.einsum('bs,bcf->scf', pick, contrib, precision=lax.Precision.HIGHEST)  49.7 us
    psum x1, waiting for transfers between devices, body(): power = lax.psum(local_power, 'chan') / jnp.float32(math.sqrt(TC))  34.8 us
    scatter x1, local copies, waits for them, and re-layouts, body(): jnp.zeros((buffer_size, BR, 2 * chan_dev), jnp.bfloat16).at[place]  33 us
    all_to_all x1, waiting for transfers between devices, body(): lax.all_to_all(gridded, 'chan', split_axis=1, concat_axis=3, tiled=True)  30.1 us
    dot_general x1, matrix products, body(): jnp.einsum('bcr,brf->bcf', got_matrix, got_vis, preferred_element_type=jn...  29 us
    reshape x1, local copies, waits for them, and re-layouts, body(): blocks = vis.reshape(nblocks, BR, 2 * chan_dev)  20.5 us
    another operation x1, other arithmetic  19.1 us
  transfers between devices with their start and end apart: 6, of which 4 were waited for; matrix products, arithmetic and copies ran while one was open for 19% of the time, Pallas kernels for 0%

commit v1 on v0

--- a/solution.py
+++ b/solution.py
@@ -79,7 +79,12 @@
     grid = jnp.einsum("bs,bcf->scf", pick, contrib, precision=lax.Precision.HIGHEST)
     gridded = grid.astype(jnp.bfloat16).reshape(slots_dev, TC, 2, chan_dev)
     table = delay_table()
-    piece = lax.all_to_all(gridded, "chan", split_axis=1, concat_axis=3, tiled=True)
+    piece = jnp.concatenate(
+        jax.lax.all_to_all(
+            jnp.stack(jnp.split(gridded, jax.lax.axis_size("chan"), axis=1), axis=0), "chan", 0, 0
+        ),
+        axis=3,
+    )
     count = piece.shape[0]
     cells_part = piece.shape[1]
     flat = piece.reshape(count * cells_part, 2 * CH)

time: 572 us -> 585 us (1.023)
  local copies, waits for them, and re-layouts: 96.4 us -> 106 us
    another operation x0 -> x5, local copies, waits for them, and re-layouts: none -> 14.7 us  [body(): jnp.stack(jnp.split(gridded, jax.lax.axis_size('chan'), axis=1), axis=0)]
    another operation x1 -> x2, other arithmetic: 19.1 us -> 22.3 us
  transfers between devices with their start and end apart: 6 -> 6, of which waited for: 4 -> 4; matrix products, arithmetic and copies ran while one was open for 19% -> 18% of each run, Pallas kernels for 0% -> 0%
where the time goes in v1:
time: 585 us; the launch traced here: 583 us
  waiting for transfers between devices  311 us (53%)
  local copies, waits for them, and re-layouts  106 us (18%)
  matrix products  89.9 us (15%)
  other arithmetic  37.5 us (6%)
  starting transfers between devices  24 us (4%)
  between operations  14.3 us (2%)
    all_to_all x1, waiting for transfers between devices, body(): lax.all_to_all(sent_vis, 'uv', split_axis=0, concat_axis=0, tiled=True)  243 us
    dot_general x1, matrix products, body(): jnp.einsum('bs,bcf->scf', pick, contrib, precision=lax.Precision.HIGHEST)  50.6 us
    psum x1, waiting for transfers between devices, body(): power = lax.psum(local_power, 'chan') / jnp.float32(math.sqrt(TC))  34.8 us
    scatter x1, local copies, waits for them, and re-layouts, body(): jnp.zeros((buffer_size, BR, 2 * chan_dev), jnp.bfloat16).at[place]  33 us
    all_to_all x1, waiting for transfers between devices, body(): jax.lax.all_to_all(jnp.stack(jnp.split(gridded, jax.lax.axis_size('chan')...  30.1 us
    dot_general x1, matrix products, body(): jnp.einsum('bcr,brf->bcf', got_matrix, got_vis, preferred_element_type=jn...  29 us
    reshape x1, local copies, waits for them, and re-layouts, body(): blocks = vis.reshape(nblocks, BR, 2 * chan_dev)  20.5 us
    another operation x1, other arithmetic  19.1 us
  transfers between devices with their start and end apart: 6, of which 4 were waited for; matrix products, arithmetic and copies ran while one was open for 18% of the time, Pallas kernels for 0%

profile of v1, /device:TPU:0, one launch (start us, length us, event | category | flops | bytes accessed | tf_op | source)
XLA Modules:
  0.0 583.0 jit_solution(230414461117738053)
XLA Ops:
  7.9 1.6 gather_fusion
  11.6 5.2 all-to-all-start
  18.2 3.1 all-to-all-done
  21.4 3.4 all-to-all-start.1
  25.5 10.6 %scatter_fusion = bf16[176,8,128]{2,1,0:T(8,128)(2,1)} fusion(bf16[176,8,128]{2,1,0:T(8,128)(2,1)} %broadcast_in_dim.144, s32[96]{0:T(128)S(1)} %fusion.47, bf16[96,8,128]{2,1,0:T(8,128)(2,1)} %bitcast.51), kind=kCustom, calls=%fused_computation.4 | custom fusion | bytes 590208 | tf_op jit(solution)/shard_map/scatter | solution.py:68
  36.1 4.1 all-to-all-start.2
  40.3 20.5 %reshape.206 = bf16[96,128,512]{2,1,0:T(8,128)(2,1)} reshape(bf16[12288,2,256]{2,1,0:T(2,128)(2,1)} %param.7) | data formatting | bytes 25165824 | tf_op jit(solution)/shard_map/reshape | solution.py:62
  60.7 7.9 %broadcast_in_dim.170 = bf16[176,128,512]{2,1,0:T(8,128)(2,1)} broadcast(bf16[]{:T(256)} %constant.24.clone.1), dimensions={} | broadcast | bytes 23068674 | tf_op jit(solution)/shard_map/broadcast_in_dim | solution.py:65
  68.6 33.0 %scatter_fusion.1 = bf16[176,128,512]{2,1,0:T(8,128)(2,1)} fusion(bf16[176,128,512]{2,1,0:T(8,128)(2,1)} %broadcast_in_dim.170, s32[96]{0:T(128)S(1)} %fusion.47, bf16[96,128,512]{2,1,0:T(8,128)(2,1)} %reshape.206), kind=kCustom, calls=%fused_computation.5 | custom fusion | bytes 37749120 | tf_op jit(solution)/shard_map/scatter | solution.py:65
  101.6 6.4 %all-to-all-start.3 = ((bf16[176,128,512]{2,1,0:T(8,128)(2,1)}), bf16[176,128,512]{2,1,0:T(8,128)(2,1)}, u32[]{:S(2)}, u32[]{:S(2)}) async-start(bf16[176,128,512]{2,1,0:T(8,128)(2,1)} %scatter_fusion.1), calls=%async_computation.3 | async-start | bytes 46137344 | tf_op jit(solution)/shard_map/all_to_all | solution.py:70
  109.3 1.6 gather_fusion.1
  110.9 5.1 broadcast_add_fusion.7
  116.6 242.7 %all-to-all-done.3 = bf16[176,128,512]{2,1,0:T(8,128)(2,1)} async-done(((bf16[176,128,512]{2,1,0:T(8,128)(2,1)}), bf16[176,128,512]{2,1,0:T(8,128)(2,1)}, u32[]{:S(2)}, u32[]{:S(2)}) %all-to-all-start.3) | async-done | bytes 23068704 | tf_op jit(solution)/shard_map/all_to_all | solution.py:70
  359.4 29.0 %fusion.9 = f32[176,128,512]{2,1,0:T(8,128)} fusion(bf16[176,128,512]{2,1,0:T(8,128)(2,1)} %all-to-all-done.3, f32[176,128]{1,0:T(8,128)S(1)} %bitcast.53, s32[176,128]{1,0:T(8,128)S(1)} %add.223, f32[176,128]{1,0:T(8,128)S(1)} %bitcast.54, s32[176,128]{1,0:T(8,128)S(1)} %add.219, f32[176,128]{1,0:T(8,128)S(1)} %bitcast.55, s32[176,128]{1,0:T(8,128)S(1)} %add.215, ...), kind=kOutput, calls=%fused_computation.28 | convolution fusion | flops 3021996032 | bytes 70647808 | tf_op jit(solution)/shard_map/bcr,brf->bcf/dot_general | solution.py:76
  388.4 50.6 %fusion.35 = bf16[19,128,512]{2,0,1:T(8,128)(2,1)} fusion(f32[176,128,512]{2,1,0:T(8,128)} %fusion.9, s32[176]{0:T(256)S(1)} %broadcast_select_fusion), kind=kOutput, calls=%fused_computation.64 | convolution fusion | flops 2631077120 | bytes 48628416 | tf_op jit(solution)/shard_map/bs,bcf->scf/dot_general | solution.py:79
  439.0 3.6 copy.14
  442.6 5.2 slice_bitcast_fusion.3
  447.8 2.2 copy.15
  450.0 2.8 copy.16
  452.8 2.8 copy.17
  455.6 1.7 copy.18
  457.3 3.2 pad_maximum_fusion
  460.5 4.9 all-to-all-start.4
  465.4 4.6 convert_element_type.65
  470.0 19.1 %multiply_convert_fusion.1 = (bf16[1024,1024]{1,0:T(8,128)(2,1)}, bf16[1024,1024]{1,0:T(8,128)(2,1)}, bf16[1024,1024]{1,0:T(8,128)(2,1)}) fusion(f32[1024]{0:T(1024)S(1)} %subtract_multiply_fusion), kind=kLoop, calls=%fused_computation.50 | loop fusion | flops 22020096 | bytes 6295552 | tf_op jit(solution)/shard_map/convert.13
  489.1 30.1 %all-to-all-done.4 = bf16[4,19,32,2,256]{4,2,3,1,0:T(8,128)(2,1)S(1)} async-done(((bf16[4,19,32,2,256]{4,2,3,1,0:T(8,128)(2,1)}), bf16[4,19,32,2,256]{4,2,3,1,0:T(8,128)(2,1)S(1)}, u32[]{:S(2)}, u32[]{:S(2)}) %all-to-all-start.4) | async-done | bytes 2490400 | tf_op jit(solution)/shard_map/all_to_all | solution.py:83
  519.2 3.6 copy.19
  522.8 4.6 dot_general.13
  527.4 10.4 %fusion.53 = (bf16[19,32,2048]{2,1,0:T(8,128)(2,1)}, f32[19,32,2048]{2,1,0:T(8,128)S(1)}) fusion(bf16[19,32,2048]{2,1,0:T(8,128)(2,1)S(1)} %dot_general.13, bf16[1024,1024]{1,0:T(8,128)(2,1)} %get-tuple-element.24, bf16[1024,1024]{1,0:T(8,128)(2,1)} %get-tuple-element.23, bf16[1024,1024]{1,0:T(8,128)(2,1)} %get-tuple-element.22), kind=kOutput, calls=%fused_computation.109 | convolution fusion | flops 5135073280 | bytes 16252928 | tf_op jit(solution)/shard_map/dot_general | solution.py:91
  537.7 2.0 fusion.34
  539.8 34.8 %all-reduce.2.cloned.1.call-done = f32[19,1024]{1,0:T(8,128)} async-done(((f32[19,1024]{1,0:T(8,128)}), f32[19,1024]{1,0:T(8,128)}) %all-reduce.2.cloned.1.call-update) | async-done | bytes 77840 | tf_op jit(solution)/shard_map/psum | solution.py:96
  574.6 1.5 broadcast_multiply_fusion
  (50 shorter events, 7.0 us)
Async XLA Ops:
  7.2 9.6 %copy-start = (s32[12288]{0:T(1024)S(1)}, s32[12288]{0:T(1024)}, u32[]{:S(2)}) copy-start(s32[12288]{0:T(1024)} %param.8) | copy-start | bytes 147460
  11.6 9.8 %all-to-all-start = ((s32[8,22,1]{1,2,0:T(1,128)}), s32[8,22,1]{1,2,0:T(1,128)S(1)}, u32[]{:S(2)}, u32[]{:S(2)}) async-start(s32[8,22,1]{1,2,0:T(1,128)} %bitcast.2), calls=%async_computation | async-start | bytes 8192 | tf_op jit(solution)/shard_map/all_to_all | solution.py:71
  21.4 14.8 %all-to-all-start.1 = ((s32[8,22,128]{2,1,0:T(8,128)}), s32[8,22,128]{2,1,0:T(8,128)S(1)}, u32[]{:S(2)}, u32[]{:S(2)}) async-start(s32[8,22,128]{2,1,0:T(8,128)} %all_to_all.23), calls=%async_computation.1 | async-start | bytes 196608 | tf_op jit(solution)/shard_map/all_to_all | solution.py:72
  36.1 65.5 %all-to-all-start.2 = ((bf16[176,8,128]{2,1,0:T(8,128)(2,1)}), bf16[176,8,128]{2,1,0:T(8,128)(2,1)S(1)}, u32[]{:S(2)}, u32[]{:S(2)}) async-start(bf16[176,8,128]{2,1,0:T(8,128)(2,1)} %scatter_fusion), calls=%async_computation.2 | async-start | bytes 720896 | tf_op jit(solution)/shard_map/all_to_all | solution.py:73
  101.6 6.5 %copy-start.2 = (s32[80]{0:T(128)S(1)}, s32[80]{0:T(128)}, u32[]{:S(2)}) copy-start(s32[80]{0:T(128)} %param.12) | copy-start | bytes 964
  101.6 6.7 %copy-start.4 = (s32[8]{0:T(128)S(1)}, s32[8]{0:T(128)}, u32[]{:S(2)}) copy-start(s32[8]{0:T(128)} %param.10) | copy-start | bytes 100
  101.6 257.8 %all-to-all-start.3 = ((bf16[176,128,512]{2,1,0:T(8,128)(2,1)}), bf16[176,128,512]{2,1,0:T(8,128)(2,1)}, u32[]{:S(2)}, u32[]{:S(2)}) async-start(bf16[176,128,512]{2,1,0:T(8,128)(2,1)} %scatter_fusion.1), calls=%async_computation.3 | async-start | bytes 46137344 | tf_op jit(solution)/shard_map/all_to_all | solution.py:70
  447.8 7.8 %copy-start.3 = (bf16[1,19,32,2,256]{2,4,3,1,0:T(8,128)(2,1)S(1)}, bf16[1,19,32,2,256]{2,4,3,1,0:T(8,128)(2,1)}, u32[]{:S(2)}) copy-start(bf16[1,19,32,2,256]{2,4,3,1,0:T(8,128)(2,1)} %get-tuple-element.3) | copy-start | bytes 1867780
  460.5 58.7 %all-to-all-start.4 = ((bf16[4,19,32,2,256]{4,2,3,1,0:T(8,128)(2,1)}), bf16[4,19,32,2,256]{4,2,3,1,0:T(8,128)(2,1)S(1)}, u32[]{:S(2)}, u32[]{:S(2)}) async-start(bf16[4,19,32,2,256]{4,2,3,1,0:T(8,128)(2,1)} %pad_maximum_fusion), calls=%async_computation.4 | async-start | bytes 4980736 | tf_op jit(solution)/shard_map/all_to_all | solution.py:83
  465.4 109.2 %all-reduce.2.cloned.1.call-start = ((), (), s32[]{:S(2)}) async-start(), calls=%async_computation.5 | async-start | bytes 196608 | tf_op jit(solution)/shard_map/psum | solution.py:96
  522.8 15.0 %slice-start = ((s8[4980736]{0:T(1024)(128)(4,1)}), s8[786432]{0:T(1024)(128)(4,1)S(1)}, s32[]{:S(2)}) async-start(s8[4980736]{0:T(1024)(128)(4,1)} %bitcast.48), calls=%async_computation.6 | async-start | bytes 1572864
  527.4 10.4 %slice-start.1 = ((s8[4980736]{0:T(1024)(128)(4,1)}), s8[4194304]{0:T(1024)(128)(4,1)S(1)}, s32[]{:S(2)}) async-start(s8[4980736]{0:T(1024)(128)(4,1)} %bitcast.48), calls=%async_computation.7 | async-start | bytes 8388608
  537.7 38.4 %copy-start.1 = (s32[12288]{0:T(1024)S(1)}, s32[12288]{0:T(1024)}, u32[]{:S(2)}) copy-start(s32[12288]{0:T(1024)} %param.8) | copy-start | bytes 147460
Sparse Core Ops, SparseCore 0:
  539.9 34.6 all-reduce.1
